TPU v7x, 512 devices: a whole 4x8x8 slice. The times are simulated.
512 devices in a mesh: dp: 64 (over z, y_hi, core), seq: 8 (over y_lo, x).
Axes of the slice: x: 4, y: 8 (y_hi: 4, y_lo: 2; y = y_hi * 2 + y_lo), z: 8, core: 2. Of those that a mesh axis runs over, the one named last changes fastest.
Arguments:
- tokens: bfloat16 [1024, 4096], P('seq', 'dp'), may hold values from -6 to 6
- in_weight: bfloat16 [2, 4096, 8192], P(None, 'seq', 'dp'), may hold values from -0.09375 to 0.09375
- conv_weight: bfloat16 [4, 8192], P(None, 'dp'), may hold values from -0.5 to 0.5
- conv_bias: bfloat16 [8192], P('dp'), may hold values from -1 to 1
- out_weight: bfloat16 [8192, 4096], P('dp', 'seq'), may hold values from -0.0625 to 0.0625
- grad_out: bfloat16 [1024, 4096], P('seq', 'dp'), may hold values from -6 to 6
Outputs:
- output: bfloat16 [1024, 4096], P('seq', 'dp')
- grad_tokens: bfloat16 [1024, 4096], P('seq', 'dp')
- grad_in_weight: float32 [2, 4096, 8192], P(None, 'seq', 'dp')
- grad_out_weight: float32 [8192, 4096], P('dp', 'seq')
- grad_conv_weight: float32 [4, 8192], P(None, 'dp')
- grad_conv_bias: float32 [8192], P('dp')
All inputs are finite; a program needn't handle non-finite values.
Results may differ from a plain program's by a relative error of at most 0.012.
Values may be sent and summed in bfloat16 or wider, within the bound.
No kernel may reach another device: no remote copies, remote signals or barrier semaphores. Data moves between devices by JAX's collectives and lax.ppermute only.
A program may use at most 64 MiB of HBM per device.

v0:
```python
import jax
import jax.numpy as jnp
from jax import lax
from jax.sharding import PartitionSpec as P

DP = ("chip", "core")


def from_behind(block, axis, distance):
    devices = range(lax.axis_size(axis))
    route = [(i - distance, i) for i in devices if i - distance in devices]
    return lax.ppermute(block, axis, route)


def silu_parts(value):
    sig = jax.nn.sigmoid(value)
    return (value * sig, sig * (1.0 + value * (1.0 - sig)))


def gather_over(block, axis, n, dim):
    rep = jnp.broadcast_to(block[None], (n,) + block.shape)
    return lax.all_to_all(rep, axis, 0, dim + 1, tiled=True)[0]


def split_exact(value):
    hi = value.astype(jnp.bfloat16)
    rest = value - hi.astype(jnp.float32)
    mid = rest.astype(jnp.bfloat16)
    lo = (rest - mid.astype(jnp.float32)).astype(jnp.bfloat16)
    return jnp.concatenate([hi, mid, lo], axis=0)


def reduce_over_dp(part, n_chip, n_core):
    split = part.astype(jnp.bfloat16)
    split = split.reshape((n_chip, n_core, part.shape[0] // (n_chip * n_core)) + part.shape[1:])
    split = lax.all_to_all(split, "core", 1, 1, tiled=True).astype(jnp.float32).sum(axis=1)
    split = split.astype(jnp.bfloat16)
    return lax.all_to_all(split, "chip", 0, 0, tiled=True).astype(jnp.float32).sum(axis=0)


def on_device(tokens, in_weight, conv_weight, conv_bias, out_weight, grad_out):
    n_seq = lax.axis_size("seq")
    n_chip = lax.axis_size("chip")
    n_core = lax.axis_size("core")
    n_dp = n_chip * n_core
    w_local = jnp.concatenate([in_weight, out_weight.T[None]], axis=0)
    w_full = lax.all_gather(w_local, "seq", axis=1, tiled=True)
    in_full = w_full[:2]
    out_full_t = w_full[2]
    acts = gather_over(jnp.stack([tokens, grad_out], axis=1), "chip", n_chip, 2)
    acts = gather_over(acts.reshape(acts.shape[:2] + (n_chip, 1, -1)), "core", n_core, 3)
    acts = acts.reshape(acts.shape[:2] + (-1,))
    whole = acts[:, 0]
    upstream = acts[:, 1]
    tok_rows = whole.shape[0]
    taps = conv_weight.shape[0]
    mixed = jnp.einsum("td,pde->tpe", whole, in_full, preferred_element_type=jnp.float32).astype(
        jnp.bfloat16
    )
    inner = mixed[:, 0, :]
    gate_in = mixed[:, 1, :]
    rim = from_behind(inner[tok_rows - (taps - 1) :], "seq", 1)
    padded = jnp.concatenate([rim, inner], axis=0)
    conv = jnp.broadcast_to(conv_bias.astype(jnp.float32)[None, :], inner.shape)
    for lag in range(taps):
        conv = conv + conv_weight[lag].astype(jnp.float32)[None, :] * padded[
            lag : lag + tok_rows
        ].astype(jnp.float32)
    act, act_slope = silu_parts(conv)
    gate, gate_slope = silu_parts(gate_in.astype(jnp.float32))
    hidden = (act * gate).astype(jnp.bfloat16)
    out_part = jnp.einsum("te,de->dt", hidden, out_full_t, preferred_element_type=jnp.float32)
    back = jnp.einsum("td,de->te", upstream, out_full_t, preferred_element_type=jnp.float32)
    grad_conv = (back * gate * act_slope).astype(jnp.bfloat16)
    grad_gate = (back * act * gate_slope).astype(jnp.bfloat16)
    ahead_rim = from_behind(grad_conv[: taps - 1], "seq", -1)
    ahead = jnp.concatenate([grad_conv, ahead_rim], axis=0)
    grad_inner = jnp.zeros(inner.shape, jnp.float32)
    for lag in range(taps):
        shift_start = taps - 1 - lag
        grad_inner = grad_inner + conv_weight[lag].astype(jnp.float32)[None, :] * ahead[
            shift_start : shift_start + tok_rows
        ].astype(jnp.float32)
    grad_inner = grad_inner.astype(jnp.bfloat16)
    conv_float = grad_conv.astype(jnp.float32)
    tap_rows = []
    for lag in range(taps):
        tap_rows.append(
            jnp.sum(conv_float * padded[lag : lag + tok_rows].astype(jnp.float32), axis=0)
        )
    conv_grads = jnp.concatenate(
        [jnp.stack(tap_rows, axis=0), jnp.sum(conv_float, axis=0)[None]], axis=0
    )
    branch_grads = jnp.stack([grad_inner, grad_gate], axis=1)
    tok_part = jnp.einsum("tpe,pde->dt", branch_grads, in_full, preferred_element_type=jnp.float32)
    reduced = reduce_over_dp(jnp.stack([out_part, tok_part], axis=1), n_chip, n_core)
    output = reduced[:, 0].T.astype(jnp.bfloat16)
    grad_tokens = reduced[:, 1].T.astype(jnp.bfloat16)
    term_in = jnp.einsum("td,tpe->pde", whole, branch_grads, preferred_element_type=jnp.float32)
    term_out_t = jnp.einsum("td,te->de", upstream, hidden, preferred_element_type=jnp.float32)
    terms = jnp.concatenate([term_in, term_out_t[None]], axis=0).astype(jnp.bfloat16)
    terms = lax.psum_scatter(terms, "seq", scatter_dimension=1, tiled=True).astype(jnp.float32)
    grad_in_weight = terms[:2]
    grad_out_weight = terms[2].T
    conv_parts = split_exact(conv_grads)
    conv_parts = jnp.broadcast_to(conv_parts[None], (n_seq,) + conv_parts.shape)
    parts = lax.all_to_all(conv_parts, "seq", 0, 0, tiled=True).astype(jnp.float32).sum(axis=0)
    n_row = taps + 1
    conv_grads = parts[:n_row] + parts[n_row : 2 * n_row] + parts[2 * n_row :]
    tap_grads = conv_grads[:taps]
    bias_grads = conv_grads[taps]
    return (output, grad_tokens, grad_in_weight, grad_out_weight, tap_grads, bias_grads)


def solution(mesh):
    n_core = 2
    devices = mesh.devices.reshape(mesh.devices.shape[0] // n_core, n_core, mesh.devices.shape[1])
    split_mesh = jax.sharding.Mesh(devices, ("chip", "core", "seq"))
    return jax.shard_map(
        on_device,
        mesh=split_mesh,
        in_specs=(P("seq", DP), P(None, "seq", DP), P(None, DP), P(DP), P(DP, "seq"), P("seq", DP)),
        out_specs=(
            P("seq", DP),
            P("seq", DP),
            P(None, "seq", DP),
            P(DP, "seq"),
            P(None, DP),
            P(DP),
        ),
        check_vma=False,
    )
```

profile of v0, /device:TPU:16, one launch (start us, length us, event | category | flops | bytes accessed | tf_op | source)
XLA Modules:
  0.0 184.7 jit_solution(6815564811677252783)
XLA Ops:
  7.2 1.0 copy.62
  8.3 1.7 pad_maximum_fusion.2
  10.0 0.7 pad_maximum_fusion.8
  10.8 1.2 broadcast_in_dim.19
  12.0 16.1 %all-to-all-start = ((bf16[32,128,2,64]{1,3,2,0:T(8,128)(2,1)}), bf16[32,128,2,64]{1,3,2,0:T(8,128)(2,1)S(1)}, u32[]{:S(2)}, u32[]{:S(2)}) async-start(bf16[32,128,2,64]{1,3,2,0:T(8,128)(2,1)} %broadcast_in_dim.19), calls=%async_computation | async-start | bytes 2097152 | tf_op jit(solution)/shard_map/all_to_all | solution.py:22
  28.2 37.0 %all-to-all-done = bf16[32,128,2,64]{1,3,2,0:T(8,128)(2,1)S(1)} async-done(((bf16[32,128,2,64]{1,3,2,0:T(8,128)(2,1)}), bf16[32,128,2,64]{1,3,2,0:T(8,128)(2,1)S(1)}, u32[]{:S(2)}, u32[]{:S(2)}) %all-to-all-start) | async-done | bytes 1048608 | tf_op jit(solution)/shard_map/all_to_all | solution.py:22
  65.2 0.6 broadcast_in_dim.21
  65.9 5.4 %all_to_all.45 = bf16[2,128,2,32,1,64]{1,5,3,2,4,0:T(8,128)(2,1)S(1)} all-to-all(bf16[2,128,2,32,1,64]{1,5,3,2,4,0:T(8,128)(2,1)S(1)} %broadcast_in_dim.21), channel_id=1, replica_groups=mesh['chip'=32,'core'=2,'seq'=8] {'core'}, dimensions={0} | all-to-all | bytes 4194304 | tf_op jit(solution)/shard_map/all_to_all | solution.py:22
  71.5 12.4 %all-gather.2.cloned.1.call-done = bf16[3,4096,128]{2,1,0:T(8,128)(2,1)} async-done(((bf16[3,512,128]{2,1,0:T(8,128)(2,1)}), bf16[3,4096,128]{2,1,0:T(8,128)(2,1)}) %all-gather.2.cloned.1.call-update) | async-done | bytes 3145744 | tf_op jit(solution)/shard_map/all_gather | solution.py:47
  83.8 2.3 %fusion.6 = bf16[128,2,128]{2,0,1:T(8,128)(2,1)S(1)} fusion(bf16[3,4096,128]{2,1,0:T(8,128)(2,1)} %all-gather.2.cloned.1.call-done, bf16[128,2,4096]{0,2,1:T(8,128)(2,1)S(1)} %bitcast.110), kind=kOutput, calls=%fused_computation.12 | convolution fusion | flops 268468224 | bytes 3211264 | tf_op jit(solution)/shard_map/td,pde->tpe/dot_general | solution.py:57
  86.2 2.4 %collective-permute-start = (bf16[3,128]{1,0:T(4,128)(2,1)S(1)}, bf16[3,128]{1,0:T(4,128)(2,1)S(1)}, u32[]{:S(2)}, u32[]{:S(2)}) collective-permute-start(bf16[3,128]{1,0:T(4,128)(2,1)S(1)} %slice_bitcast_fusion.11), channel_id=1, source_target_pairs={{0,1},{1,2},{2,3},{3,4},{4,5},{5,6},{6,7},{8,9},{9,10},{10,11},{11... | collective-permute-start | bytes 2312 | tf_op jit(solution)/shard_map/ppermute | solution.py:12
  88.5 1.3 collective-permute-done
  90.4 1.3 collective-permute-start.1
  92.2 3.9 %collective-permute-done.1 = bf16[3,128]{1,0:T(4,128)(2,1)S(1)} collective-permute-done((bf16[3,128]{1,0:T(4,128)(2,1)S(1)}, bf16[3,128]{1,0:T(4,128)(2,1)S(1)}, u32[]{:S(2)}, u32[]{:S(2)}) %collective-permute-start.1) | collective-permute-done | bytes 800 | tf_op jit(solution)/shard_map/ppermute | solution.py:12
  96.1 0.7 fusion
  96.9 2.0 %pad_maximum_fusion = bf16[3,4096,128]{1,2,0:T(8,128)(2,1)} fusion(bf16[1,4096,128]{1,2,0:T(8,128)(2,1)S(1)} %fusion.2, bf16[2,4096,128]{1,2,0:T(8,128)(2,1)S(1)} %fusion), kind=kLoop, calls=%fused_computation.6 | loop fusion | flops 1572864 | bytes 6291456 | tf_op jit(solution)/shard_map/concatenate | solution.py:101
  98.9 1.1 slice-done
  100.5 2.3 %fusion.1 = bf16[4096,128]{1,0:T(8,128)(2,1)S(1)} fusion(bf16[3,4096,128]{2,1,0:T(8,128)(2,1)} %all-gather.2.cloned.1.call-done, bf16[128,1,128]{2,0,1:T(8,128)(2,1)S(1)} %fusion.34, bf16[128,1,128]{2,0,1:T(8,128)(2,1)S(1)} %fusion.35), kind=kOutput, calls=%fused_computation.3 | convolution fusion | flops 269090816 | bytes 4259840 | tf_op jit(solution)/shard_map/tpe,pde->dt/dot_general | solution.py:95
  103.2 5.4 %all_to_all.46 = bf16[32,2,64,2,128]{4,2,0,3,1:T(8,128)(2,1)S(1)} all-to-all(bf16[32,2,64,2,128]{4,2,0,3,1:T(8,128)(2,1)S(1)} %copy.66), channel_id=1, replica_groups=mesh['chip'=32,'core'=2,'seq'=8] {'core'}, dimensions={1} | all-to-all | bytes 4194304 | tf_op jit(solution)/shard_map/all_to_all | solution.py:36
  108.7 0.6 broadcast_in_dim.24
  109.3 6.5 %all-to-all-start.4 = ((bf16[8,15,128]{2,1,0:T(8,128)(2,1)}), bf16[8,15,128]{2,1,0:T(8,128)(2,1)S(1)}, u32[]{:S(2)}, u32[]{:S(2)}) async-start(bf16[8,15,128]{2,1,0:T(8,128)(2,1)} %broadcast_in_dim.24), calls=%async_computation.5 | async-start | bytes 65536 | tf_op jit(solution)/shard_map/all_to_all | solution.py:107
  115.8 0.6 reduce_sum.75
  116.4 1.1 copy.68
  117.5 4.6 %all-to-all-done.4 = bf16[8,15,128]{2,1,0:T(8,128)(2,1)S(1)} async-done(((bf16[8,15,128]{2,1,0:T(8,128)(2,1)}), bf16[8,15,128]{2,1,0:T(8,128)(2,1)S(1)}, u32[]{:S(2)}, u32[]{:S(2)}) %all-to-all-start.4) | async-done | bytes 30752 | tf_op jit(solution)/shard_map/all_to_all | solution.py:107
  122.1 12.3 %all-to-all-start.3 = ((bf16[32,64,2,128]{3,1,2,0:T(8,128)(2,1)}), bf16[32,64,2,128]{3,1,2,0:T(8,128)(2,1)S(1)}, u32[]{:S(2)}, u32[]{:S(2)}) async-start(bf16[32,64,2,128]{3,1,2,0:T(8,128)(2,1)} %copy.68), calls=%async_computation.3 | async-start | bytes 2097152 | tf_op jit(solution)/shard_map/all_to_all | solution.py:38
  134.4 0.6 slice.120
  135.5 36.3 %all-to-all-done.3 = bf16[32,64,2,128]{3,1,2,0:T(8,128)(2,1)S(1)} async-done(((bf16[32,64,2,128]{3,1,2,0:T(8,128)(2,1)}), bf16[32,64,2,128]{3,1,2,0:T(8,128)(2,1)S(1)}, u32[]{:S(2)}, u32[]{:S(2)}) %all-to-all-start.3) | async-done | bytes 1048608 | tf_op jit(solution)/shard_map/all_to_all | solution.py:38
  172.0 0.6 slice_bitcast_fusion.9
  172.6 2.4 %reduce-scatter.2.cloned.1.call-done = bf16[3,512,128]{1,2,0:T(8,128)(2,1)} async-done(((bf16[3,4096,128]{1,2,0:T(8,128)(2,1)}), bf16[3,512,128]{1,2,0:T(8,128)(2,1)}) %reduce-scatter.2.cloned.1.call-update) | async-done | bytes 393232 | tf_op jit(solution)/shard_map/reduce_scatter | solution.py:102
  175.0 1.1 slice.140
  176.1 1.0 copy.72
  177.2 0.7 slice_bitcast_fusion.6
  (35 shorter events, 3.2 us)
Async XLA Ops:
  7.2 76.6 %all-gather.2.cloned.1.call-start = ((), (), s32[]{:S(2)}) async-start(), calls=%async_computation.6 | async-start | bytes 3538944 | tf_op jit(solution)/shard_map/all_gather | solution.py:47
  8.2 19.9 %copy-start.3 = (bf16[128]{0:T(256)(128)(2,1)S(1)}, bf16[128]{0:T(256)(128)(2,1)}, u32[]{:S(2)}) copy-start(bf16[128]{0:T(256)(128)(2,1)} %param.9) | copy-start | bytes 772
  8.2 19.9 %copy-start.2 = (bf16[4,128]{1,0:T(4,128)(2,1)S(1)}, bf16[4,128]{1,0:T(4,128)(2,1)}, u32[]{:S(2)}) copy-start(bf16[4,128]{1,0:T(4,128)(2,1)} %param.8) | copy-start | bytes 3076
  12.0 53.1 %all-to-all-start = ((bf16[32,128,2,64]{1,3,2,0:T(8,128)(2,1)}), bf16[32,128,2,64]{1,3,2,0:T(8,128)(2,1)S(1)}, u32[]{:S(2)}, u32[]{:S(2)}) async-start(bf16[32,128,2,64]{1,3,2,0:T(8,128)(2,1)} %broadcast_in_dim.19), calls=%async_computation | async-start | bytes 2097152 | tf_op jit(solution)/shard_map/all_to_all | solution.py:22
  28.1 146.9 %reduce-scatter.2.cloned.1.call-start = ((), (), s32[]{:S(2)}) async-start(), calls=%async_computation.7 | async-start | bytes 3538944 | tf_op jit(solution)/shard_map/reduce_scatter | solution.py:102
  83.8 6.0 %copy-start = (bf16[3,4096,128]{2,1,0:T(8,128)(2,1)S(1)}, bf16[3,4096,128]{2,1,0:T(8,128)(2,1)}, u32[]{:S(2)}) copy-start(bf16[3,4096,128]{2,1,0:T(8,128)(2,1)} %all-gather.2.cloned.1.call-done) | copy-start | bytes 9437188
  86.2 3.7 %collective-permute-start = (bf16[3,128]{1,0:T(4,128)(2,1)S(1)}, bf16[3,128]{1,0:T(4,128)(2,1)S(1)}, u32[]{:S(2)}, u32[]{:S(2)}) collective-permute-start(bf16[3,128]{1,0:T(4,128)(2,1)S(1)} %slice_bitcast_fusion.11), channel_id=1, source_target_pairs={{0,1},{1,2},{2,3},{3,4},{4,5},{5,6},{6,7},{8,9},{9,10},{10,11},{11... | collective-permute-start | bytes 2312 | tf_op jit(solution)/shard_map/ppermute | solution.py:12
  90.4 5.7 %collective-permute-start.1 = (bf16[3,128]{1,0:T(4,128)(2,1)S(1)}, bf16[3,128]{1,0:T(4,128)(2,1)S(1)}, u32[]{:S(2)}, u32[]{:S(2)}) collective-permute-start(bf16[3,128]{1,0:T(4,128)(2,1)S(1)} %slice.133), channel_id=1, source_target_pairs={{1,0},{2,1},{3,2},{4,3},{5,4},{6,5},{7,6},{9,8},{10,9},{11,10},{12... | collective-permute-start | bytes 2312 | tf_op jit(solution)/shard_map/ppermute | solution.py:12
  98.8 1.2 slice-start
  109.3 12.9 %all-to-all-start.4 = ((bf16[8,15,128]{2,1,0:T(8,128)(2,1)}), bf16[8,15,128]{2,1,0:T(8,128)(2,1)S(1)}, u32[]{:S(2)}, u32[]{:S(2)}) async-start(bf16[8,15,128]{2,1,0:T(8,128)(2,1)} %broadcast_in_dim.24), calls=%async_computation.5 | async-start | bytes 65536 | tf_op jit(solution)/shard_map/all_to_all | solution.py:107
  122.1 49.7 %all-to-all-start.3 = ((bf16[32,64,2,128]{3,1,2,0:T(8,128)(2,1)}), bf16[32,64,2,128]{3,1,2,0:T(8,128)(2,1)S(1)}, u32[]{:S(2)}, u32[]{:S(2)}) async-start(bf16[32,64,2,128]{3,1,2,0:T(8,128)(2,1)} %copy.68), calls=%async_computation.3 | async-start | bytes 2097152 | tf_op jit(solution)/shard_map/all_to_all | solution.py:38
  175.0 2.1 %copy-start.1 = (bf16[3,512,128]{1,2,0:T(8,128)(2,1)S(1)}, bf16[3,512,128]{1,2,0:T(8,128)(2,1)}, u32[]{:S(2)}) copy-start(bf16[3,512,128]{1,2,0:T(8,128)(2,1)} %reduce-scatter.2.cloned.1.call-done) | copy-start | bytes 1179652
Sparse Core Ops, SparseCore 0:
  10.7 73.1 all-gather.1
  99.0 75.9 reduce-scatter.1
where the time goes:
time: 185 us
  waiting for transfers between devices  97.8 us (53%)
  starting transfers between devices  38.6 us (21%)
  between operations  14.3 us (8%)
  local copies, waits for them, and re-layouts  10.8 us (6%)
  blocking collectives  10.8 us (6%)
  matrix products  6.81 us (4%)
  other arithmetic  5.69 us (3%)
    all_to_all x1, waiting for transfers between devices, gather_over(): return lax.all_to_all(rep, axis, 0, dim + 1, tiled=True)[0]  37 us
    all_to_all x1, waiting for transfers between devices, reduce_over_dp(): lax.all_to_all(split, 'chip', 0, 0, tiled=True).astype(jnp.float32)  36.3 us
    all_to_all x1, starting transfers between devices, gather_over(): return lax.all_to_all(rep, axis, 0, dim + 1, tiled=True)[0]  16.1 us
    all_gather x1, waiting for transfers between devices, on_device(): w_full = lax.all_gather(w_local, 'seq', axis=1, tiled=True)  12.4 us
    all_to_all x1, starting transfers between devices, reduce_over_dp(): lax.all_to_all(split, 'chip', 0, 0, tiled=True).astype(jnp.float32)  12.3 us
    all_to_all x1, starting transfers between devices, on_device(): lax.all_to_all(conv_parts, 'seq', 0, 0, tiled=True).astype(jnp.float32)  6.5 us
    all_to_all x1, blocking collectives, gather_over(): return lax.all_to_all(rep, axis, 0, dim + 1, tiled=True)[0]  5.42 us
    all_to_all x1, blocking collectives, reduce_over_dp(): lax.all_to_all(split, 'core', 1, 1, tiled=True).astype(jnp.float32)  5.42 us
  transfers between devices with their start and end apart: 7, of which 7 were waited for; matrix products, arithmetic and copies ran while one was open for 6% of the time, Pallas kernels for 0%

commit v1 on v0

--- a/solution.py
+++ b/solution.py
@@ -44,7 +44,9 @@
     n_core = lax.axis_size("core")
     n_dp = n_chip * n_core
     w_local = jnp.concatenate([in_weight, out_weight.T[None]], axis=0)
-    w_full = lax.all_gather(w_local, "seq", axis=1, tiled=True)
+    w_full = jnp.concatenate(
+        lax.all_to_all(jnp.stack(lax.axis_size("seq") * [w_local], 0), "seq", 0, 0), axis=1
+    )
     in_full = w_full[:2]
     out_full_t = w_full[2]
     acts = gather_over(jnp.stack([tokens, grad_out], axis=1), "chip", n_chip, 2)

time: 185 us -> 207 us (1.12)
  the two profiles are of different devices: /device:TPU:16 before, /device:TPU:40 now
where the time goes in v1:
time: 207 us; the launch traced here: 206 us
  waiting for transfers between devices  112 us (54%)
  starting transfers between devices  42.5 us (21%)
  local copies, waits for them, and re-layouts  18.1 us (9%)
  between operations  14.3 us (7%)
  blocking collectives  11.7 us (6%)
  other arithmetic  3.99 us (2%)
  matrix products  3.48 us (2%)
    all_to_all x1, waiting for transfers between devices, reduce_over_dp(): lax.all_to_all(split, 'chip', 0, 0, tiled=True).astype(jnp.float32)  35 us
    all_to_all x1, waiting for transfers between devices, on_device(): lax.all_to_all(jnp.stack(lax.axis_size('seq') * [w_local], 0), 'seq', 0, 0)  33.8 us
    all_to_all x1, waiting for transfers between devices, gather_over(): return lax.all_to_all(rep, axis, 0, dim + 1, tiled=True)[0]  27.4 us
    all_to_all x1, starting transfers between devices, gather_over(): return lax.all_to_all(rep, axis, 0, dim + 1, tiled=True)[0]  15.8 us
    all_to_all x1, starting transfers between devices, reduce_over_dp(): lax.all_to_all(split, 'chip', 0, 0, tiled=True).astype(jnp.float32)  9.25 us
    all_to_all x1, starting transfers between devices, on_device(): lax.all_to_all(jnp.stack(lax.axis_size('seq') * [w_local], 0), 'seq', 0, 0)  8.79 us
    ppermute x2, waiting for transfers between devices, from_behind(): return lax.ppermute(block, axis, route)  7.66 us
    all_to_all x1, blocking collectives, gather_over(): return lax.all_to_all(rep, axis, 0, dim + 1, tiled=True)[0]  6.31 us
  transfers between devices with their start and end apart: 7, of which 7 were waited for; matrix products, arithmetic and copies ran while one was open for 5% of the time, Pallas kernels for 0%

profile of v1, /device:TPU:40, one launch (start us, length us, event | category | flops | bytes accessed | tf_op | source)
XLA Modules:
  0.0 205.9 jit_solution(4717775127092235895)
XLA Ops:
  7.2 0.8 pad_maximum_fusion.8
  8.0 1.2 broadcast_in_dim.19
  9.2 15.8 %all-to-all-start.1 = ((bf16[32,128,2,64]{1,3,2,0:T(8,128)(2,1)}), bf16[32,128,2,64]{1,3,2,0:T(8,128)(2,1)S(1)}, u32[]{:S(2)}, u32[]{:S(2)}) async-start(bf16[32,128,2,64]{1,3,2,0:T(8,128)(2,1)} %broadcast_in_dim.19), calls=%async_computation.1 | async-start | bytes 2097152 | tf_op jit(solution)/shard_map/all_to_all | solution.py:22
  25.3 27.4 %all-to-all-done.1 = bf16[32,128,2,64]{1,3,2,0:T(8,128)(2,1)S(1)} async-done(((bf16[32,128,2,64]{1,3,2,0:T(8,128)(2,1)}), bf16[32,128,2,64]{1,3,2,0:T(8,128)(2,1)S(1)}, u32[]{:S(2)}, u32[]{:S(2)}) %all-to-all-start.1) | async-done | bytes 1048608 | tf_op jit(solution)/shard_map/all_to_all | solution.py:22
  52.7 0.6 broadcast_in_dim.21
  53.4 6.3 %all_to_all.50 = bf16[2,128,2,32,1,64]{1,5,3,2,4,0:T(8,128)(2,1)} all-to-all(bf16[2,128,2,32,1,64]{1,5,3,2,4,0:T(8,128)(2,1)S(1)} %broadcast_in_dim.21), channel_id=1, replica_groups=mesh['chip'=32,'core'=2,'seq'=8] {'core'}, dimensions={0} | all-to-all | bytes 4194304 | tf_op jit(solution)/shard_map/all_to_all | solution.py:22
  59.7 2.3 %stack.46 = bf16[8,3,512,128]{3,2,1,0:T(8,128)(2,1)} broadcast(bf16[3,512,128]{2,1,0:T(8,128)(2,1)S(1)} %pad_maximum_fusion.2), dimensions={1,2,3} | broadcast | bytes 3538944 | tf_op jit(solution)/shard_map/stack | solution.py:48
  62.0 8.8 %all-to-all-start = ((bf16[8,3,512,128]{3,2,1,0:T(8,128)(2,1)}), bf16[8,3,512,128]{3,2,1,0:T(8,128)(2,1)S(1)}, u32[]{:S(2)}, u32[]{:S(2)}) async-start(bf16[8,3,512,128]{3,2,1,0:T(8,128)(2,1)} %stack.46), calls=%async_computation | async-start | bytes 6291456 | tf_op jit(solution)/shard_map/all_to_all | solution.py:48
  70.8 3.2 %copy.74 = bf16[2,128,2,32,1,64]{1,5,0,3,2,4:T(8,128)(2,1)} copy(bf16[2,128,2,32,1,64]{1,5,3,2,4,0:T(8,128)(2,1)} %all_to_all.50) | data formatting | bytes 4194304 | tf_op jit(solution)/shard_map/all_to_all | solution.py:22
  74.0 33.8 %all-to-all-done = bf16[8,3,512,128]{3,2,1,0:T(8,128)(2,1)S(1)} async-done(((bf16[8,3,512,128]{3,2,1,0:T(8,128)(2,1)}), bf16[8,3,512,128]{3,2,1,0:T(8,128)(2,1)S(1)}, u32[]{:S(2)}, u32[]{:S(2)}) %all-to-all-start) | async-done | bytes 3145760 | tf_op jit(solution)/shard_map/all_to_all | solution.py:48
  108.2 2.1 %copy-done = bf16[2,128,2,32,1,64]{1,5,0,3,2,4:T(8,128)(2,1)S(1)} copy-done((bf16[2,128,2,32,1,64]{1,5,0,3,2,4:T(8,128)(2,1)S(1)}, bf16[2,128,2,32,1,64]{1,5,0,3,2,4:T(8,128)(2,1)}, u32[]{:S(2)}) %copy-start) | copy-done | bytes 2097176
  110.9 2.8 %collective-permute-start = (bf16[3,128]{1,0:T(4,128)(2,1)S(1)}, bf16[3,128]{1,0:T(4,128)(2,1)S(1)}, u32[]{:S(2)}, u32[]{:S(2)}) collective-permute-start(bf16[3,128]{1,0:T(4,128)(2,1)S(1)} %slice_bitcast_fusion.11), channel_id=1, source_target_pairs={{0,1},{1,2},{2,3},{3,4},{4,5},{5,6},{6,7},{8,9},{9,10},{10,11},{11... | collective-permute-start | bytes 2312 | tf_op jit(solution)/shard_map/ppermute | solution.py:12
  113.8 4.7 %collective-permute-done = bf16[3,128]{1,0:T(4,128)(2,1)S(1)} collective-permute-done((bf16[3,128]{1,0:T(4,128)(2,1)S(1)}, bf16[3,128]{1,0:T(4,128)(2,1)S(1)}, u32[]{:S(2)}, u32[]{:S(2)}) %collective-permute-start) | collective-permute-done | bytes 800 | tf_op jit(solution)/shard_map/ppermute | solution.py:12
  119.0 1.9 collective-permute-start.1
  121.5 3.0 %collective-permute-done.1 = bf16[3,128]{1,0:T(4,128)(2,1)S(1)} collective-permute-done((bf16[3,128]{1,0:T(4,128)(2,1)S(1)}, bf16[3,128]{1,0:T(4,128)(2,1)S(1)}, u32[]{:S(2)}, u32[]{:S(2)}) %collective-permute-start.1) | collective-permute-done | bytes 800 | tf_op jit(solution)/shard_map/ppermute | solution.py:12
  124.5 0.7 fusion
  125.3 1.9 pad_maximum_fusion
  127.3 1.1 copy-done.2
  129.1 0.7 fusion.4
  130.4 5.4 %all_to_all.51 = bf16[32,2,64,2,128]{4,2,0,3,1:T(8,128)(2,1)S(1)} all-to-all(bf16[32,2,64,2,128]{4,2,0,3,1:T(8,128)(2,1)S(1)} %copy.79), channel_id=1, replica_groups=mesh['chip'=32,'core'=2,'seq'=8] {'core'}, dimensions={1} | all-to-all | bytes 4194304 | tf_op jit(solution)/shard_map/all_to_all | solution.py:36
  135.8 0.6 broadcast_in_dim.24
  136.4 4.0 %all-to-all-start.5 = ((bf16[8,15,128]{2,1,0:T(8,128)(2,1)}), bf16[8,15,128]{2,1,0:T(8,128)(2,1)S(1)}, u32[]{:S(2)}, u32[]{:S(2)}) async-start(bf16[8,15,128]{2,1,0:T(8,128)(2,1)} %broadcast_in_dim.24), calls=%async_computation.6 | async-start | bytes 65536 | tf_op jit(solution)/shard_map/all_to_all | solution.py:109
  140.4 0.6 reduce_sum.75
  141.0 1.1 copy.81
  142.1 3.2 %all-to-all-done.5 = bf16[8,15,128]{2,1,0:T(8,128)(2,1)S(1)} async-done(((bf16[8,15,128]{2,1,0:T(8,128)(2,1)}), bf16[8,15,128]{2,1,0:T(8,128)(2,1)S(1)}, u32[]{:S(2)}, u32[]{:S(2)}) %all-to-all-start.5) | async-done | bytes 30752 | tf_op jit(solution)/shard_map/all_to_all | solution.py:109
  145.3 9.2 %all-to-all-start.4 = ((bf16[32,64,2,128]{3,1,2,0:T(8,128)(2,1)}), bf16[32,64,2,128]{3,1,2,0:T(8,128)(2,1)S(1)}, u32[]{:S(2)}, u32[]{:S(2)}) async-start(bf16[32,64,2,128]{3,1,2,0:T(8,128)(2,1)} %copy.81), calls=%async_computation.4 | async-start | bytes 2097152 | tf_op jit(solution)/shard_map/all_to_all | solution.py:38
  155.7 35.0 %all-to-all-done.4 = bf16[32,64,2,128]{3,1,2,0:T(8,128)(2,1)S(1)} async-done(((bf16[32,64,2,128]{3,1,2,0:T(8,128)(2,1)}), bf16[32,64,2,128]{3,1,2,0:T(8,128)(2,1)S(1)}, u32[]{:S(2)}, u32[]{:S(2)}) %all-to-all-start.4) | async-done | bytes 1048608 | tf_op jit(solution)/shard_map/all_to_all | solution.py:38
  190.8 0.6 slice_bitcast_fusion.9
  191.4 4.7 %reduce-scatter.2.cloned.1.call-done = bf16[3,512,128]{1,2,0:T(8,128)(2,1)} async-done(((bf16[3,4096,128]{1,2,0:T(8,128)(2,1)}), bf16[3,512,128]{1,2,0:T(8,128)(2,1)}) %reduce-scatter.2.cloned.1.call-update) | async-done | bytes 393232 | tf_op jit(solution)/shard_map/reduce_scatter | solution.py:104
  196.1 1.1 slice.145
  197.2 1.0 copy.85
  198.3 0.7 slice_bitcast_fusion.6
  (49 shorter events, 5.0 us)
Async XLA Ops:
  7.2 17.9 %copy-start.7 = (bf16[128,512]{1,0:T(8,128)(2,1)S(1)}, bf16[128,512]{1,0:T(8,128)(2,1)}, u32[]{:S(2)}) copy-start(bf16[128,512]{1,0:T(8,128)(2,1)} %param.10) | copy-start | bytes 393220
  7.2 18.0 %copy-start.6 = (bf16[2,512,128]{2,1,0:T(8,128)(2,1)S(1)}, bf16[2,512,128]{2,1,0:T(8,128)(2,1)}, u32[]{:S(2)}) copy-start(bf16[2,512,128]{2,1,0:T(8,128)(2,1)} %param.7) | copy-start | bytes 786436
  9.2 43.4 %all-to-all-start.1 = ((bf16[32,128,2,64]{1,3,2,0:T(8,128)(2,1)}), bf16[32,128,2,64]{1,3,2,0:T(8,128)(2,1)S(1)}, u32[]{:S(2)}, u32[]{:S(2)}) async-start(bf16[32,128,2,64]{1,3,2,0:T(8,128)(2,1)} %broadcast_in_dim.19), calls=%async_computation.1 | async-start | bytes 2097152 | tf_op jit(solution)/shard_map/all_to_all | solution.py:22
  62.0 8.8 %copy-start.9 = (bf16[128]{0:T(256)(128)(2,1)S(1)}, bf16[128]{0:T(256)(128)(2,1)}, u32[]{:S(2)}) copy-start(bf16[128]{0:T(256)(128)(2,1)} %param.9) | copy-start | bytes 772
  62.0 8.8 %copy-start.8 = (bf16[4,128]{1,0:T(4,128)(2,1)S(1)}, bf16[4,128]{1,0:T(4,128)(2,1)}, u32[]{:S(2)}) copy-start(bf16[4,128]{1,0:T(4,128)(2,1)} %param.8) | copy-start | bytes 3076
  62.0 45.8 %all-to-all-start = ((bf16[8,3,512,128]{3,2,1,0:T(8,128)(2,1)}), bf16[8,3,512,128]{3,2,1,0:T(8,128)(2,1)S(1)}, u32[]{:S(2)}, u32[]{:S(2)}) async-start(bf16[8,3,512,128]{3,2,1,0:T(8,128)(2,1)} %stack.46), calls=%async_computation | async-start | bytes 6291456 | tf_op jit(solution)/shard_map/all_to_all | solution.py:48
  70.8 125.3 %reduce-scatter.2.cloned.1.call-start = ((), (), s32[]{:S(2)}) async-start(), calls=%async_computation.7 | async-start | bytes 3538944 | tf_op jit(solution)/shard_map/reduce_scatter | solution.py:104
  108.0 2.3 %copy-start = (bf16[2,128,2,32,1,64]{1,5,0,3,2,4:T(8,128)(2,1)S(1)}, bf16[2,128,2,32,1,64]{1,5,0,3,2,4:T(8,128)(2,1)}, u32[]{:S(2)}) copy-start(bf16[2,128,2,32,1,64]{1,5,0,3,2,4:T(8,128)(2,1)} %copy.74) | copy-start | bytes 6291460
  108.2 5.6 %copy-start.4 = (bf16[2,8,512,128]{3,2,1,0:T(8,128)(2,1)}, bf16[2,8,512,128]{3,2,1,0:T(8,128)(2,1)S(1)}, u32[]{:S(2)}) copy-start(bf16[2,8,512,128]{3,2,1,0:T(8,128)(2,1)S(1)} %copy.76) | copy-start | bytes 6291460
  110.9 7.6 %collective-permute-start = (bf16[3,128]{1,0:T(4,128)(2,1)S(1)}, bf16[3,128]{1,0:T(4,128)(2,1)S(1)}, u32[]{:S(2)}, u32[]{:S(2)}) collective-permute-start(bf16[3,128]{1,0:T(4,128)(2,1)S(1)} %slice_bitcast_fusion.11), channel_id=1, source_target_pairs={{0,1},{1,2},{2,3},{3,4},{4,5},{5,6},{6,7},{8,9},{9,10},{10,11},{11... | collective-permute-start | bytes 2312 | tf_op jit(solution)/shard_map/ppermute | solution.py:12
  113.8 4.7 %copy-start.1 = (bf16[1,8,512,128]{3,2,0,1:T(8,128)(2,1)}, bf16[1,8,512,128]{3,2,0,1:T(8,128)(2,1)S(1)}, u32[]{:S(2)}) copy-start(bf16[1,8,512,128]{3,2,0,1:T(8,128)(2,1)S(1)} %slice.127) | copy-start | bytes 3145732
  119.0 5.5 %collective-permute-start.1 = (bf16[3,128]{1,0:T(4,128)(2,1)S(1)}, bf16[3,128]{1,0:T(4,128)(2,1)S(1)}, u32[]{:S(2)}, u32[]{:S(2)}) collective-permute-start(bf16[3,128]{1,0:T(4,128)(2,1)S(1)} %slice.138), channel_id=1, source_target_pairs={{1,0},{2,1},{3,2},{4,3},{5,4},{6,5},{7,6},{9,8},{10,9},{11,10},{12... | collective-permute-start | bytes 2312 | tf_op jit(solution)/shard_map/ppermute | solution.py:12
  127.2 1.2 copy-start.2
  127.2 1.9 copy-start.5
  136.4 8.9 %all-to-all-start.5 = ((bf16[8,15,128]{2,1,0:T(8,128)(2,1)}), bf16[8,15,128]{2,1,0:T(8,128)(2,1)S(1)}, u32[]{:S(2)}, u32[]{:S(2)}) async-start(bf16[8,15,128]{2,1,0:T(8,128)(2,1)} %broadcast_in_dim.24), calls=%async_computation.6 | async-start | bytes 65536 | tf_op jit(solution)/shard_map/all_to_all | solution.py:109
  145.3 45.4 %all-to-all-start.4 = ((bf16[32,64,2,128]{3,1,2,0:T(8,128)(2,1)}), bf16[32,64,2,128]{3,1,2,0:T(8,128)(2,1)S(1)}, u32[]{:S(2)}, u32[]{:S(2)}) async-start(bf16[32,64,2,128]{3,1,2,0:T(8,128)(2,1)} %copy.81), calls=%async_computation.4 | async-start | bytes 2097152 | tf_op jit(solution)/shard_map/all_to_all | solution.py:38
  196.1 2.1 %copy-start.3 = (bf16[3,512,128]{1,2,0:T(8,128)(2,1)S(1)}, bf16[3,512,128]{1,2,0:T(8,128)(2,1)}, u32[]{:S(2)}) copy-start(bf16[3,512,128]{1,2,0:T(8,128)(2,1)} %reduce-scatter.2.cloned.1.call-done) | copy-start | bytes 1179652
Sparse Core Ops, SparseCore 0:
  127.4 68.7 reduce-scatter.1
